TPU v7x, 512 devices: a whole 4x8x8 slice. The times are simulated.
512 devices in a mesh: member: 16 (over x_lo, y), dp: 32 (over z, x_hi, core).
Axes of the slice: x: 4 (x_hi: 2, x_lo: 2; x = x_hi * 2 + x_lo), y: 8, z: 8, core: 2. Of those that a mesh axis runs over, the one named last changes fastest.
Arguments:
- inputs: bfloat16 [8192, 64], P('dp'), may hold values from -6 to 6
- observed: float32 [64, 8192], P('member', 'dp'), may hold values from -6 to 6
- noise: bfloat16 [2, 32, 64, 8192], P(None, None, 'member', 'dp'), may hold values from -4 to 4
- w_in: float32 [32, 64, 4096], P('member', None, 'dp'), may hold values from -0.75 to 0.75
- b_in: float32 [32, 4096], P('member', 'dp'), may hold values from -3 to 3
- w_out: float32 [32, 64, 4096], P('member', None, 'dp'), may hold values from -0.09375 to 0.09375
- b_out: float32 [32, 64], P('member'), may hold values from -3 to 3
Outputs:
- new_w_in: float32 [32, 64, 4096], P('member', None, 'dp')
- new_b_in: float32 [32, 4096], P('member', 'dp')
- new_w_out: float32 [32, 64, 4096], P('member', None, 'dp')
- new_b_out: float32 [32, 64], P('member')
All inputs are finite; a program needn't handle non-finite values.
Results may differ from a plain program's by a relative error of at most 0.00056.
Values may be sent and summed in bfloat16 or wider, within the bound.
No kernel may reach another device: no remote copies, remote signals or barrier semaphores. Data moves between devices by JAX's collectives and lax.ppermute only.
A program may use at most 64 MiB of HBM per device.

v0:
```python
import jax
import jax.numpy as jnp
from jax import lax
from jax.sharding import PartitionSpec as P

UPDATES = 2
ridge_level = 0.5


def solve_gain(gram, cross):
    eye = jnp.eye(gram.shape[0], dtype=gram.dtype)
    factor = jnp.linalg.cholesky(gram + ridge_level * eye)
    middle = lax.linalg.triangular_solve(factor, cross, left_side=True, lower=True)
    return lax.linalg.triangular_solve(factor, middle, left_side=True, lower=True, transpose_a=True)


def predict(inputs, w_in, b_in, w_out, b_out):
    shards = (
        w_in.astype(jnp.bfloat16),
        w_out.astype(jnp.bfloat16),
        b_in.astype(jnp.bfloat16)[:, None, :],
    )

    def single(item):
        weight_in, weight_out, bias_in = item
        pre = jnp.dot(inputs, weight_in, preferred_element_type=jnp.float32) + bias_in.astype(
            jnp.float32
        )
        hidden = jnp.tanh(pre).astype(jnp.bfloat16)
        return lax.dot_general(
            weight_out, hidden, (((1,), (1,)), ((), ())), preferred_element_type=jnp.float32
        )

    total = lax.map(
        single,
        (
            lax.all_gather(shards[0], "dp", axis=2, tiled=True),
            lax.all_gather(shards[1], "dp", axis=2, tiled=True),
            lax.all_gather(shards[2], "dp", axis=2, tiled=True),
        ),
    )
    return total + b_out[:, :, None]


def mix_own(own, whole, columns):
    flat = whole.reshape(whole.shape[0], -1)
    moved = lax.dot_general(
        columns, flat, (((0,), (0,)), ((), ())), precision=lax.Precision.HIGHEST
    )
    return own + moved.reshape(own.shape)


def on_device(inputs, observed, noise, w_in, b_in, w_out, b_out):
    per_device = w_in.shape[0]
    count = observed.shape[0] * lax.axis_size("member") * observed.shape[1] * lax.axis_size("dp")
    for update in range(UPDATES):
        predicted = predict(inputs, w_in, b_in, w_out, b_out)
        collected = lax.all_to_all(
            predicted.astype(jnp.bfloat16), "member", split_axis=1, concat_axis=0, tiled=True
        ).astype(predicted.dtype)
        mean_pred = jnp.mean(collected, axis=0)
        anomaly = (collected - mean_pred[None]).reshape(collected.shape[0], -1)
        misfit = (observed[None] + noise[update].astype(jnp.float32) - collected).reshape(
            collected.shape[0], -1
        )
        gram_part = lax.dot_general(
            anomaly, anomaly, (((1,), (1,)), ((), ())), precision=lax.Precision.HIGHEST
        )
        cross_part = lax.dot_general(
            anomaly, misfit, (((1,), (1,)), ((), ())), precision=lax.Precision.HIGHEST
        )
        gram, cross = lax.psum((gram_part, cross_part), ("member", "dp"))
        gain = solve_gain(gram / count, cross / count)
        whole_in, whole_bias, whole_out, whole_bout = (
            lax.all_gather(w_in, "member", axis=0, tiled=True),
            lax.all_gather(b_in, "member", axis=0, tiled=True),
            lax.all_gather(w_out, "member", axis=0, tiled=True),
            lax.all_gather(b_out, "member", axis=0, tiled=True),
        )
        first = lax.axis_index("member") * per_device
        columns = lax.dynamic_slice_in_dim(gain, first, per_device, 1)
        w_in = mix_own(w_in, whole_in, columns)
        b_in = mix_own(b_in, whole_bias, columns)
        w_out = mix_own(w_out, whole_out, columns)
        b_out = mix_own(b_out, whole_bout, columns)
    return (w_in, b_in, w_out, b_out)


def solution(mesh):
    placed = (
        P("dp", None),
        P("member", "dp"),
        P(None, None, "member", "dp"),
        P("member", None, "dp"),
        P("member", "dp"),
        P("member", None, "dp"),
        P("member", None),
    )
    return jax.shard_map(
        on_device,
        mesh=mesh,
        in_specs=placed,
        out_specs=(
            P("member", None, "dp"),
            P("member", "dp"),
            P("member", None, "dp"),
            P("member", None),
        ),
        check_vma=False,
    )
```

profile of v0, /device:TPU:1, one launch (start us, length us, event | category | flops | bytes accessed | tf_op | source)
XLA Modules:
  0.0 656.1 jit_solution(13720734547421046891)
XLA Ops:
  7.2 1.5 convert_element_type.118
  8.7 1.5 convert_element_type.119
  10.3 0.7 all-gather.21.cloned.1.call-update
  11.0 0.7 convert_element_type.120
  11.7 48.9 %all-gather = bf16[2,4096]{1,0:T(2,128)(2,1)S(1)} all-gather(bf16[2,128]{1,0:T(2,128)(2,1)S(1)} %convert_element_type.120), channel_id=2, replica_groups=mesh['member'=16,'dp'=32] {'dp'}, dimensions={1}, use_global_device_ids=true | all-gather | bytes 16896 | tf_op jit(solution)/shard_map/all_gather | solution.py:39
  60.6 35.2 %all-gather.15.cloned.1.call-done = bf16[2,64,4096]{2,1,0:T(8,128)(2,1)} async-done(((bf16[2,64,128]{2,1,0:T(8,128)(2,1)}), bf16[2,64,4096]{2,1,0:T(8,128)(2,1)}) %all-gather.15.cloned.1.call-update) | async-done | bytes 1048592 | tf_op jit(solution)/shard_map/all_gather | solution.py:38
  95.8 79.4 %all-gather.17.cloned.1.call-done = bf16[2,64,4096]{2,1,0:T(8,128)(2,1)} async-done(((bf16[2,64,128]{2,1,0:T(8,128)(2,1)}), bf16[2,64,4096]{2,1,0:T(8,128)(2,1)}) %all-gather.17.cloned.1.call-update) | async-done | bytes 1048592 | tf_op jit(solution)/shard_map/all_gather | solution.py:37
  175.2 5.3 while.20
  175.3 2.6 fusion.92
  177.9 2.6 fusion.92
  180.6 0.7 copy.79
  181.3 6.6 %all-to-all-start = ((bf16[2,64,256]{2,0,1:T(2,128)(2,1)}), bf16[2,64,256]{2,0,1:T(2,128)(2,1)S(1)}, u32[]{:S(2)}, u32[]{:S(2)}) async-start(bf16[2,64,256]{2,0,1:T(2,128)(2,1)} %copy.79), calls=%async_computation | async-start | bytes 131072 | tf_op jit(solution)/shard_map/all_to_all | solution.py:58
  188.0 0.5 all-gather.19.cloned.1.call-update
  188.5 6.8 %all-to-all-done = bf16[2,64,256]{2,0,1:T(2,128)(2,1)S(1)} async-done(((bf16[2,64,256]{2,0,1:T(2,128)(2,1)}), bf16[2,64,256]{2,0,1:T(2,128)(2,1)S(1)}, u32[]{:S(2)}, u32[]{:S(2)}) %all-to-all-start) | async-done | bytes 65568 | tf_op jit(solution)/shard_map/all_to_all | solution.py:58
  196.3 98.6 %all-reduce.1 = (f32[32,32]{0,1:T(8,128)S(1)}, f32[32,32]{0,1:T(8,128)S(1)}) all-reduce(f32[32,32]{0,1:T(8,128)S(1)} %convolution_bitcast_fusion.3, f32[32,32]{0,1:T(8,128)S(1)} %convolution_bitcast_fusion.2), channel_id=1, replica_groups=mesh['member'=16,'dp'=32] {'member','dp'}, use_global_device_ids=true, to_apply=%region_3.4 | all-reduce | flops 2048 | bytes 16384 | tf_op jit(solution)/shard_map/psum | solution.py:72
  294.9 2.9 cholesky.44
  297.9 0.6 compare_reduce_fusion.1
  298.5 0.7 fusion.42
  299.2 2.4 custom-call.11
  302.1 3.0 fusion.64
  305.2 2.2 all-gather.19.cloned.1.call-done
  307.4 3.0 fusion.65
  310.4 24.5 %all-gather.3 = f32[16,2,64]{2,1,0:T(2,128)S(1)} all-gather(f32[1,2,64]{2,1,0:T(2,128)S(1)} %bitcast.235), channel_id=1, replica_groups=mesh['member'=16,'dp'=32] {'member'}, dimensions={0}, use_global_device_ids=true | all-gather | bytes 8704 | tf_op jit(solution)/shard_map/all_gather | solution.py:78
  334.9 22.7 %all-gather.2 = f32[16,2,128]{2,1,0:T(2,128)S(1)} all-gather(f32[1,2,128]{2,1,0:T(2,128)S(1)} %bitcast.237), channel_id=1, replica_groups=mesh['member'=16,'dp'=32] {'member'}, dimensions={0}, use_global_device_ids=true | all-gather | bytes 17408 | tf_op jit(solution)/shard_map/all_gather | solution.py:76
  357.6 0.6 copy.102
  358.5 67.2 %all-gather.1 = bf16[2,4096]{1,0:T(2,128)(2,1)S(1)} all-gather(bf16[2,128]{1,0:T(2,128)(2,1)S(1)} %get-tuple-element.163), channel_id=3, replica_groups=mesh['member'=16,'dp'=32] {'dp'}, dimensions={1}, use_global_device_ids=true | all-gather | bytes 16896 | tf_op jit(solution)/shard_map/all_gather | solution.py:39
  425.8 1.8 copy.90
  427.7 32.0 %all-gather.25.cloned.1.call-done = bf16[2,64,4096]{2,0,1:T(2,128)(2,1)} async-done(((bf16[2,64,128]{2,0,1:T(2,128)(2,1)}), bf16[2,64,4096]{2,0,1:T(2,128)(2,1)}) %all-gather.25.cloned.1.call-update) | async-done | bytes 1048592 | tf_op jit(solution)/shard_map/all_gather | solution.py:37
  459.6 1.8 copy.91
  461.5 2.9 while.21
  461.5 1.4 fusion.96
  462.9 1.4 fusion.96
  464.4 0.7 copy.93
  465.1 7.3 %all-to-all-start.1 = ((bf16[2,64,256]{2,0,1:T(2,128)(2,1)}), bf16[2,64,256]{2,0,1:T(2,128)(2,1)S(1)}, u32[]{:S(2)}, u32[]{:S(2)}) async-start(bf16[2,64,256]{2,0,1:T(2,128)(2,1)} %copy.93), calls=%async_computation.1 | async-start | bytes 131072 | tf_op jit(solution)/shard_map/all_to_all | solution.py:58
  472.5 0.6 copy.100
  473.2 27.3 %all-gather.5 = f32[16,2,64]{2,1,0:T(2,128)S(1)} all-gather(f32[1,2,64]{2,1,0:T(2,128)S(1)} %bitcast.234), channel_id=1, replica_groups=mesh['member'=16,'dp'=32] {'member'}, dimensions={0}, use_global_device_ids=true | all-gather | bytes 8704 | tf_op jit(solution)/shard_map/all_gather | solution.py:78
  500.4 23.3 %all-gather.4 = f32[16,2,128]{2,1,0:T(2,128)S(1)} all-gather(f32[1,2,128]{2,1,0:T(2,128)S(1)} %bitcast.236), channel_id=1, replica_groups=mesh['member'=16,'dp'=32] {'member'}, dimensions={0}, use_global_device_ids=true | all-gather | bytes 17408 | tf_op jit(solution)/shard_map/all_gather | solution.py:76
  524.7 109.9 %all-reduce = (f32[32,32]{0,1:T(8,128)S(1)}, f32[32,32]{0,1:T(8,128)S(1)}) all-reduce(f32[32,32]{0,1:T(8,128)S(1)} %convolution_bitcast_fusion.1, f32[32,32]{0,1:T(8,128)S(1)} %convolution_bitcast_fusion), channel_id=1, replica_groups=mesh['member'=16,'dp'=32] {'member','dp'}, use_global_device_ids=true, to_apply=%region_10.14 | all-reduce | flops 2048 | bytes 16384 | tf_op jit(solution)/shard_map/psum | solution.py:72
  634.7 2.9 cholesky.55
  637.6 0.6 compare_reduce_fusion
  638.3 0.7 fusion.43
  638.9 2.4 custom-call.13
  641.9 2.4 convolution_add_fusion.2
  644.2 0.6 copy.105
  644.9 0.7 convolution_add_fusion.6
  645.6 0.7 convolution_add_fusion.7
  646.3 2.4 convolution_add_fusion.3
  648.7 0.6 copy.104
  (75 shorter events, 4.0 us)
Async XLA Ops:
  7.2 88.7 %all-gather.15.cloned.1.call-start = ((), (), s32[]{:S(2)}) async-start(), calls=%async_computation.2 | async-start | bytes 1081344 | tf_op jit(solution)/shard_map/all_gather | solution.py:38
  8.7 166.5 %all-gather.17.cloned.1.call-start = ((), (), s32[]{:S(2)}) async-start(), calls=%async_computation.3 | async-start | bytes 1081344 | tf_op jit(solution)/shard_map/all_gather | solution.py:37
  10.2 291.9 %all-gather.21.cloned.1.call-start = ((), (), s32[]{:S(2)}) async-start(), calls=%async_computation.5 | async-start | bytes 1114112 | tf_op jit(solution)/shard_map/all_gather | solution.py:77
  175.2 5.3 copy-start.4
  180.5 15.4 %copy-start.2 = (bf16[2,32,4,256]{3,2,1,0:T(4,128)(2,1)S(1)}, bf16[2,32,4,256]{3,2,1,0:T(4,128)(2,1)}, u32[]{:S(2)}) copy-start(bf16[2,32,4,256]{3,2,1,0:T(4,128)(2,1)} %param.18) | copy-start | bytes 393220
  180.5 15.4 %copy-start.3 = (f32[4,256]{1,0:T(4,128)S(1)}, f32[4,256]{1,0:T(4,128)}, u32[]{:S(2)}) copy-start(f32[4,256]{1,0:T(4,128)} %param.17) | copy-start | bytes 12292
  181.3 14.0 %all-to-all-start = ((bf16[2,64,256]{2,0,1:T(2,128)(2,1)}), bf16[2,64,256]{2,0,1:T(2,128)(2,1)S(1)}, u32[]{:S(2)}, u32[]{:S(2)}) async-start(bf16[2,64,256]{2,0,1:T(2,128)(2,1)} %copy.79), calls=%async_computation | async-start | bytes 131072 | tf_op jit(solution)/shard_map/all_to_all | solution.py:58
  187.9 119.4 %all-gather.19.cloned.1.call-start = ((), (), s32[]{:S(2)}) async-start(), calls=%async_computation.4 | async-start | bytes 1114112 | tf_op jit(solution)/shard_map/all_gather | solution.py:75
  188.5 237.3 %all-gather.23.cloned.1.call-start = ((), (), s32[]{:S(2)}) async-start(), calls=%async_computation.6 | async-start | bytes 1081344 | tf_op jit(solution)/shard_map/all_gather | solution.py:38
  195.4 106.7 %copy-start = (f32[2,64,128]{2,1,0:T(8,128)S(1)}, f32[2,64,128]{2,1,0:T(8,128)}, u32[]{:S(2)}) copy-start(f32[2,64,128]{2,1,0:T(8,128)} %param.21) | copy-start | bytes 196612
  196.0 111.4 %copy-start.1 = (f32[2,64,128]{2,1,0:T(8,128)S(1)}, f32[2,64,128]{2,1,0:T(8,128)}, u32[]{:S(2)}) copy-start(f32[2,64,128]{2,1,0:T(8,128)} %param.19) | copy-start | bytes 196612
  302.1 32.8 %copy-start.5 = (f32[2,128]{1,0:T(2,128)S(1)}, f32[2,128]{1,0:T(2,128)}, u32[]{:S(2)}) copy-start(f32[2,128]{1,0:T(2,128)} %param.20) | copy-start | bytes 3076
  305.1 154.5 %all-gather.25.cloned.1.call-start = ((), (), s32[]{:S(2)}) async-start(), calls=%async_computation.7 | async-start | bytes 1081344 | tf_op jit(solution)/shard_map/all_gather | solution.py:37
  310.4 331.5 %all-gather.29.cloned.1.call-start = ((), (), s32[]{:S(2)}) async-start(), calls=%async_computation.9 | async-start | bytes 1114112 | tf_op jit(solution)/shard_map/all_gather | solution.py:77
  427.6 33.8 %copy-start.6 = (bf16[256,64]{0,1:T(8,128)(2,1)S(1)}, bf16[256,64]{0,1:T(8,128)(2,1)}, u32[]{:S(2)}) copy-start(bf16[256,64]{0,1:T(8,128)(2,1)} %get-tuple-element.315) | copy-start | bytes 98308
  465.1 58.6 %all-to-all-start.1 = ((bf16[2,64,256]{2,0,1:T(2,128)(2,1)}), bf16[2,64,256]{2,0,1:T(2,128)(2,1)S(1)}, u32[]{:S(2)}, u32[]{:S(2)}) async-start(bf16[2,64,256]{2,0,1:T(2,128)(2,1)} %copy.93), calls=%async_computation.1 | async-start | bytes 131072 | tf_op jit(solution)/shard_map/all_to_all | solution.py:58
  472.4 173.9 %all-gather.27.cloned.1.call-start = ((), (), s32[]{:S(2)}) async-start(), calls=%async_computation.8 | async-start | bytes 1114112 | tf_op jit(solution)/shard_map/all_gather | solution.py:75
Sparse Core Ops, SparseCore 0:
  11.7 84.0 all-gather.14
  99.5 75.6 all-gather.16
  177.3 58.8 all-gather.20
  238.1 69.2 all-gather.18
  310.9 76.3 all-gather.22
  390.8 68.7 all-gather.24
  461.7 62.1 all-gather.28
  526.5 68.6 all-gather.26
where the time goes:
time: 657 us; the launch traced here: 656 us
  blocking collectives  422 us (64%)
  waiting for transfers between devices  157 us (24%)
  matrix products  22.2 us (3%)
  other arithmetic  17.7 us (3%)
  between operations  14.5 us (2%)
  starting transfers between devices  14.2 us (2%)
  local copies, waits for them, and re-layouts  8.08 us (1%)
    psum x2, blocking collectives, on_device(): gram, cross = lax.psum((gram_part, cross_part), ('member', 'dp'))  208 us
    all_gather x2, blocking collectives, predict(): lax.all_gather(shards[2], 'dp', axis=2, tiled=True)  116 us
    all_gather x2, waiting for transfers between devices, predict(): lax.all_gather(shards[0], 'dp', axis=2, tiled=True)  111 us
    all_gather x2, blocking collectives, on_device(): lax.all_gather(b_out, 'member', axis=0, tiled=True)  51.8 us
    all_gather x2, blocking collectives, on_device(): lax.all_gather(b_in, 'member', axis=0, tiled=True)  46 us
    all_gather x2, waiting for transfers between devices, predict(): lax.all_gather(shards[1], 'dp', axis=2, tiled=True)  35.2 us
    all_to_all x2, starting transfers between devices, on_device(): lax.all_to_all(predicted.astype(jnp.bfloat16), 'member', split_axis=1, co...  13.8 us
  transfers between devices with their start and end apart: 10, of which 5 were waited for; matrix products, arithmetic and copies ran while one was open for 7% of the time, Pallas kernels for 0%

commit v1 on v0

--- a/solution.py
+++ b/solution.py
@@ -5,6 +5,10 @@
 
 UPDATES = 2
 ridge_level = 0.5
+_set_panel = lambda sample: jnp.concatenate(
+    lax.all_to_all(jnp.stack([sample] * lax.axis_size("dp")), "dp", concat_axis=0, split_axis=0),
+    axis=2,
+)
 
 
 def solve_gain(gram, cross):
@@ -36,7 +40,7 @@
         (
             lax.all_gather(shards[0], "dp", axis=2, tiled=True),
             lax.all_gather(shards[1], "dp", axis=2, tiled=True),
-            lax.all_gather(shards[2], "dp", axis=2, tiled=True),
+            _set_panel(shards[2]),
         ),
     )
     return total + b_out[:, :, None]

time: 657 us -> 657 us (level)
  blocking collectives: 422 us -> 306 us
  waiting for transfers between devices: 157 us -> 223 us
  starting transfers between devices: 14.2 us -> 63.5 us
    all_gather x2 -> x0, blocking collectives: 116 us -> none  [predict(): lax.all_gather(shards[2], 'dp', axis=2, tiled=True)]
    all_to_all x0 -> x2, starting transfers between devices: none -> 49.3 us  [lax.all_to_all(jnp.stack([sample] * lax.axis_size('dp')), 'dp', concat_ax...]
    all_gather x2, waiting for transfers between devices: 111 us -> 143 us  [predict(): lax.all_gather(shards[0], 'dp', axis=2, tiled=True)]
    all_gather x2, waiting for transfers between devices: 35.2 us -> 59.8 us  [predict(): lax.all_gather(shards[1], 'dp', axis=2, tiled=True)]
    all_to_all x0 -> x2, waiting for transfers between devices: none -> 9.36 us  [lax.all_to_all(jnp.stack([sample] * lax.axis_size('dp')), 'dp', concat_ax...]
  transfers between devices with their start and end apart: 10 -> 12, of which waited for: 5 -> 6; matrix products, arithmetic and copies ran while one was open for 7% -> 7% of each run, Pallas kernels for 0% -> 0%
where the time goes in v1:
time: 657 us; the launch traced here: 656 us
  blocking collectives  306 us (47%)
  waiting for transfers between devices  223 us (34%)
  starting transfers between devices  63.5 us (10%)
  matrix products  22.2 us (3%)
  other arithmetic  17.7 us (3%)
  between operations  14.5 us (2%)
  local copies, waits for them, and re-layouts  9.29 us (1%)
    psum x2, blocking collectives, on_device(): gram, cross = lax.psum((gram_part, cross_part), ('member', 'dp'))  207 us
    all_gather x2, waiting for transfers between devices, predict(): lax.all_gather(shards[0], 'dp', axis=2, tiled=True)  143 us
    all_gather x2, waiting for transfers between devices, predict(): lax.all_gather(shards[1], 'dp', axis=2, tiled=True)  59.8 us
    all_gather x2, blocking collectives, on_device(): lax.all_gather(b_out, 'member', axis=0, tiled=True)  51.9 us
    all_to_all x2, starting transfers between devices, lax.all_to_all(jnp.stack([sample] * lax.axis_size('dp')), 'dp', concat_ax...  49.3 us
    all_gather x2, blocking collectives, on_device(): lax.all_gather(b_in, 'member', axis=0, tiled=True)  46.9 us
    all_to_all x2, starting transfers between devices, on_device(): lax.all_to_all(predicted.astype(jnp.bfloat16), 'member', split_axis=1, co...  13.8 us
  transfers between devices with their start and end apart: 12, of which 6 were waited for; matrix products, arithmetic and copies ran while one was open for 7% of the time, Pallas kernels for 0%

profile of v1, /device:TPU:1, one launch (start us, length us, event | category | flops | bytes accessed | tf_op | source)
XLA Modules:
  0.0 656.0 jit_solution(5785491708035342888)
XLA Ops:
  7.2 1.5 convert_element_type.118
  8.7 1.5 convert_element_type.119
  10.3 0.7 all-gather.19.cloned.1.call-update
  11.0 0.7 convert_element_type.120
  12.3 14.4 %all-to-all-start = ((bf16[32,2,1,128]{3,1,2,0:T(2,128)(2,1)}), bf16[32,2,1,128]{3,1,2,0:T(2,128)(2,1)S(1)}, u32[]{:S(2)}, u32[]{:S(2)}) async-start(bf16[32,2,1,128]{3,1,2,0:T(2,128)(2,1)} %stack.6), calls=%async_computation | async-start | bytes 32768 | tf_op jit(solution)/shard_map/all_to_all | solution.py:9
  26.7 9.4 %all-to-all-done = bf16[32,2,1,128]{3,1,2,0:T(2,128)(2,1)S(1)} async-done(((bf16[32,2,1,128]{3,1,2,0:T(2,128)(2,1)}), bf16[32,2,1,128]{3,1,2,0:T(2,128)(2,1)S(1)}, u32[]{:S(2)}, u32[]{:S(2)}) %all-to-all-start) | async-done | bytes 16416 | tf_op jit(solution)/shard_map/all_to_all | solution.py:9
  36.1 59.8 %all-gather.13.cloned.1.call-done = bf16[2,64,4096]{2,1,0:T(8,128)(2,1)} async-done(((bf16[2,64,128]{2,1,0:T(8,128)(2,1)}), bf16[2,64,4096]{2,1,0:T(8,128)(2,1)}) %all-gather.13.cloned.1.call-update) | async-done | bytes 1048592 | tf_op jit(solution)/shard_map/all_gather | solution.py:42
  95.8 79.4 %all-gather.15.cloned.1.call-done = bf16[2,64,4096]{2,1,0:T(8,128)(2,1)} async-done(((bf16[2,64,128]{2,1,0:T(8,128)(2,1)}), bf16[2,64,4096]{2,1,0:T(8,128)(2,1)}) %all-gather.15.cloned.1.call-update) | async-done | bytes 1048592 | tf_op jit(solution)/shard_map/all_gather | solution.py:41
  175.2 5.3 while.20
  175.3 2.6 fusion.92
  177.9 2.6 fusion.92
  180.6 0.7 copy.78
  181.3 6.6 %all-to-all-start.1 = ((bf16[2,64,256]{2,0,1:T(2,128)(2,1)}), bf16[2,64,256]{2,0,1:T(2,128)(2,1)S(1)}, u32[]{:S(2)}, u32[]{:S(2)}) async-start(bf16[2,64,256]{2,0,1:T(2,128)(2,1)} %copy.78), calls=%async_computation.1 | async-start | bytes 131072 | tf_op jit(solution)/shard_map/all_to_all | solution.py:62
  188.5 6.8 %all-to-all-done.1 = bf16[2,64,256]{2,0,1:T(2,128)(2,1)S(1)} async-done(((bf16[2,64,256]{2,0,1:T(2,128)(2,1)}), bf16[2,64,256]{2,0,1:T(2,128)(2,1)S(1)}, u32[]{:S(2)}, u32[]{:S(2)}) %all-to-all-start.1) | async-done | bytes 65568 | tf_op jit(solution)/shard_map/all_to_all | solution.py:62
  196.3 98.5 %all-reduce.1 = (f32[32,32]{0,1:T(8,128)S(1)}, f32[32,32]{0,1:T(8,128)S(1)}) all-reduce(f32[32,32]{0,1:T(8,128)S(1)} %convolution_bitcast_fusion.3, f32[32,32]{0,1:T(8,128)S(1)} %convolution_bitcast_fusion.2), channel_id=1, replica_groups=mesh['member'=16,'dp'=32] {'member','dp'}, use_global_device_ids=true, to_apply=%region_3.4 | all-reduce | flops 2048 | bytes 16384 | tf_op jit(solution)/shard_map/psum | solution.py:76
  294.9 2.9 cholesky.44
  297.8 0.6 compare_reduce_fusion.1
  298.5 0.7 fusion.42
  299.1 2.4 custom-call.11
  302.1 3.0 fusion.64
  305.2 2.2 all-gather.17.cloned.1.call-done
  307.3 3.0 fusion.65
  310.4 24.7 %all-gather.1 = f32[16,2,64]{2,1,0:T(2,128)S(1)} all-gather(f32[1,2,64]{2,1,0:T(2,128)S(1)} %bitcast.239), channel_id=1, replica_groups=mesh['member'=16,'dp'=32] {'member'}, dimensions={0}, use_global_device_ids=true | all-gather | bytes 8704 | tf_op jit(solution)/shard_map/all_gather | solution.py:82
  335.1 22.7 %all-gather = f32[16,2,128]{2,1,0:T(2,128)S(1)} all-gather(f32[1,2,128]{2,1,0:T(2,128)S(1)} %bitcast.241), channel_id=1, replica_groups=mesh['member'=16,'dp'=32] {'member'}, dimensions={0}, use_global_device_ids=true | all-gather | bytes 17408 | tf_op jit(solution)/shard_map/all_gather | solution.py:80
  357.7 0.6 copy.101
  359.1 34.9 %all-to-all-start.2 = ((bf16[32,2,1,128]{3,1,2,0:T(2,128)(2,1)}), bf16[32,2,1,128]{3,1,2,0:T(2,128)(2,1)S(1)}, u32[]{:S(2)}, u32[]{:S(2)}) async-start(bf16[32,2,1,128]{3,1,2,0:T(2,128)(2,1)} %stack.7), calls=%async_computation.2 | async-start | bytes 32768 | tf_op jit(solution)/shard_map/all_to_all | solution.py:9
  394.1 1.8 copy.89
  396.0 63.8 %all-gather.23.cloned.1.call-done = bf16[2,64,4096]{2,0,1:T(2,128)(2,1)} async-done(((bf16[2,64,128]{2,0,1:T(2,128)(2,1)}), bf16[2,64,4096]{2,0,1:T(2,128)(2,1)}) %all-gather.23.cloned.1.call-update) | async-done | bytes 1048592 | tf_op jit(solution)/shard_map/all_gather | solution.py:41
  459.8 1.8 copy.90
  461.6 2.9 while.21
  461.6 1.4 fusion.96
  463.1 1.4 fusion.96
  464.6 0.7 copy.92
  465.3 7.3 %all-to-all-start.3 = ((bf16[2,64,256]{2,0,1:T(2,128)(2,1)}), bf16[2,64,256]{2,0,1:T(2,128)(2,1)S(1)}, u32[]{:S(2)}, u32[]{:S(2)}) async-start(bf16[2,64,256]{2,0,1:T(2,128)(2,1)} %copy.92), calls=%async_computation.3 | async-start | bytes 131072 | tf_op jit(solution)/shard_map/all_to_all | solution.py:62
  472.6 0.6 copy.99
  473.3 27.3 %all-gather.3 = f32[16,2,64]{2,1,0:T(2,128)S(1)} all-gather(f32[1,2,64]{2,1,0:T(2,128)S(1)} %bitcast.238), channel_id=1, replica_groups=mesh['member'=16,'dp'=32] {'member'}, dimensions={0}, use_global_device_ids=true | all-gather | bytes 8704 | tf_op jit(solution)/shard_map/all_gather | solution.py:82
  500.6 24.3 %all-gather.2 = f32[16,2,128]{2,1,0:T(2,128)S(1)} all-gather(f32[1,2,128]{2,1,0:T(2,128)S(1)} %bitcast.240), channel_id=1, replica_groups=mesh['member'=16,'dp'=32] {'member'}, dimensions={0}, use_global_device_ids=true | all-gather | bytes 17408 | tf_op jit(solution)/shard_map/all_gather | solution.py:80
  525.8 108.7 %all-reduce = (f32[32,32]{0,1:T(8,128)S(1)}, f32[32,32]{0,1:T(8,128)S(1)}) all-reduce(f32[32,32]{0,1:T(8,128)S(1)} %convolution_bitcast_fusion.1, f32[32,32]{0,1:T(8,128)S(1)} %convolution_bitcast_fusion), channel_id=1, replica_groups=mesh['member'=16,'dp'=32] {'member','dp'}, use_global_device_ids=true, to_apply=%region_10.14 | all-reduce | flops 2048 | bytes 16384 | tf_op jit(solution)/shard_map/psum | solution.py:76
  634.6 2.9 cholesky.55
  637.5 0.6 compare_reduce_fusion
  638.1 0.7 fusion.43
  638.8 2.4 custom-call.13
  641.7 2.4 convolution_add_fusion.2
  644.1 0.6 copy.104
  644.7 0.7 convolution_add_fusion.6
  645.4 0.7 convolution_add_fusion.7
  646.1 2.4 convolution_add_fusion.3
  648.5 0.6 copy.103
  (79 shorter events, 5.7 us)
Async XLA Ops:
  7.2 88.7 %all-gather.13.cloned.1.call-start = ((), (), s32[]{:S(2)}) async-start(), calls=%async_computation.4 | async-start | bytes 1081344 | tf_op jit(solution)/shard_map/all_gather | solution.py:42
  8.7 166.5 %all-gather.15.cloned.1.call-start = ((), (), s32[]{:S(2)}) async-start(), calls=%async_computation.5 | async-start | bytes 1081344 | tf_op jit(solution)/shard_map/all_gather | solution.py:41
  10.2 291.8 %all-gather.19.cloned.1.call-start = ((), (), s32[]{:S(2)}) async-start(), calls=%async_computation.7 | async-start | bytes 1114112 | tf_op jit(solution)/shard_map/all_gather | solution.py:81
  12.3 23.8 %all-to-all-start = ((bf16[32,2,1,128]{3,1,2,0:T(2,128)(2,1)}), bf16[32,2,1,128]{3,1,2,0:T(2,128)(2,1)S(1)}, u32[]{:S(2)}, u32[]{:S(2)}) async-start(bf16[32,2,1,128]{3,1,2,0:T(2,128)(2,1)} %stack.6), calls=%async_computation | async-start | bytes 32768 | tf_op jit(solution)/shard_map/all_to_all | solution.py:9
  175.2 5.3 copy-start.4
  180.5 15.4 %copy-start.2 = (bf16[2,32,4,256]{3,2,1,0:T(4,128)(2,1)S(1)}, bf16[2,32,4,256]{3,2,1,0:T(4,128)(2,1)}, u32[]{:S(2)}) copy-start(bf16[2,32,4,256]{3,2,1,0:T(4,128)(2,1)} %param.18) | copy-start | bytes 393220
  180.5 15.4 %copy-start.3 = (f32[4,256]{1,0:T(4,128)S(1)}, f32[4,256]{1,0:T(4,128)}, u32[]{:S(2)}) copy-start(f32[4,256]{1,0:T(4,128)} %param.17) | copy-start | bytes 12292
  181.3 14.0 %all-to-all-start.1 = ((bf16[2,64,256]{2,0,1:T(2,128)(2,1)}), bf16[2,64,256]{2,0,1:T(2,128)(2,1)S(1)}, u32[]{:S(2)}, u32[]{:S(2)}) async-start(bf16[2,64,256]{2,0,1:T(2,128)(2,1)} %copy.78), calls=%async_computation.1 | async-start | bytes 131072 | tf_op jit(solution)/shard_map/all_to_all | solution.py:62
  187.9 119.4 %all-gather.17.cloned.1.call-start = ((), (), s32[]{:S(2)}) async-start(), calls=%async_computation.6 | async-start | bytes 1114112 | tf_op jit(solution)/shard_map/all_gather | solution.py:79
  188.5 205.7 %all-gather.21.cloned.1.call-start = ((), (), s32[]{:S(2)}) async-start(), calls=%async_computation.8 | async-start | bytes 1081344 | tf_op jit(solution)/shard_map/all_gather | solution.py:42
  195.4 106.6 %copy-start = (f32[2,64,128]{2,1,0:T(8,128)S(1)}, f32[2,64,128]{2,1,0:T(8,128)}, u32[]{:S(2)}) copy-start(f32[2,64,128]{2,1,0:T(8,128)} %param.21) | copy-start | bytes 196612
  195.9 111.4 %copy-start.1 = (f32[2,64,128]{2,1,0:T(8,128)S(1)}, f32[2,64,128]{2,1,0:T(8,128)}, u32[]{:S(2)}) copy-start(f32[2,64,128]{2,1,0:T(8,128)} %param.19) | copy-start | bytes 196612
  302.1 33.0 %copy-start.5 = (f32[2,128]{1,0:T(2,128)S(1)}, f32[2,128]{1,0:T(2,128)}, u32[]{:S(2)}) copy-start(f32[2,128]{1,0:T(2,128)} %param.20) | copy-start | bytes 3076
  305.1 154.7 %all-gather.23.cloned.1.call-start = ((), (), s32[]{:S(2)}) async-start(), calls=%async_computation.9 | async-start | bytes 1081344 | tf_op jit(solution)/shard_map/all_gather | solution.py:41
  310.3 331.4 %all-gather.27.cloned.1.call-start = ((), (), s32[]{:S(2)}) async-start(), calls=%async_computation.11 | async-start | bytes 1114112 | tf_op jit(solution)/shard_map/all_gather | solution.py:81
  359.1 102.4 %all-to-all-start.2 = ((bf16[32,2,1,128]{3,1,2,0:T(2,128)(2,1)}), bf16[32,2,1,128]{3,1,2,0:T(2,128)(2,1)S(1)}, u32[]{:S(2)}, u32[]{:S(2)}) async-start(bf16[32,2,1,128]{3,1,2,0:T(2,128)(2,1)} %stack.7), calls=%async_computation.2 | async-start | bytes 32768 | tf_op jit(solution)/shard_map/all_to_all | solution.py:9
  396.0 65.6 %copy-start.6 = (bf16[256,64]{0,1:T(8,128)(2,1)S(1)}, bf16[256,64]{0,1:T(8,128)(2,1)}, u32[]{:S(2)}) copy-start(bf16[256,64]{0,1:T(8,128)(2,1)} %get-tuple-element.317) | copy-start | bytes 98308
  465.3 59.6 %all-to-all-start.3 = ((bf16[2,64,256]{2,0,1:T(2,128)(2,1)}), bf16[2,64,256]{2,0,1:T(2,128)(2,1)S(1)}, u32[]{:S(2)}, u32[]{:S(2)}) async-start(bf16[2,64,256]{2,0,1:T(2,128)(2,1)} %copy.92), calls=%async_computation.3 | async-start | bytes 131072 | tf_op jit(solution)/shard_map/all_to_all | solution.py:62
  472.5 173.6 %all-gather.25.cloned.1.call-start = ((), (), s32[]{:S(2)}) async-start(), calls=%async_computation.10 | async-start | bytes 1114112 | tf_op jit(solution)/shard_map/all_gather | solution.py:79
Sparse Core Ops, SparseCore 0:
  11.7 84.0 all-gather.12
  99.5 75.6 all-gather.14
  177.3 58.8 all-gather.18
  238.1 69.1 all-gather.16
  310.8 76.3 all-gather.20
  390.8 68.8 all-gather.22
  461.8 61.3 all-gather.26
  525.8 69.5 all-gather.24
